TPU v7x, 128 devices: a whole 4x4x4 slice. The times are simulated.
128 devices in a mesh: outer: 16 (over z, x), inner: 8 (over y, core).
Axes of the slice: x: 4, y: 4, z: 4, core: 2. Of those that a mesh axis runs over, the one named last changes fastest.
Arguments:
- features: bfloat16 [4194304, 64], P(('outer', 'inner')), may hold values from -6 to 6
- block_offset: int32 [32768], P(('outer', 'inner')), may hold values from 0 to 7
- parent_entry: int32 [4194304], P(('outer', 'inner')), may hold values from 0 to 8191, as said below
- owner_cell: int32 [128, 8192], P(('outer', 'inner')), may hold values from 0 to 4096, as said below
- w_down: bfloat16 [8, 64, 128], replicated, may hold values from -0.25 to 0.25
- b_down: float32 [128], replicated, may hold values from -3 to 3
- w_up: bfloat16 [8, 128, 64], replicated, may hold values from -0.5 to 0.5
Outputs:
- refined: bfloat16 [4194304, 64], P(('outer', 'inner'))
Inputs may be any that keep to these rules, and one draw needn't show every extreme that they name: `parent_entry`: In each group the first c slots are used (1 <= c <= 512), the rest empty; group 7 and one more group have all 512 slots used on every device. A voxel names a used entry of its own device; all voxels of one brick of 128 name entries of one aligned window of 128 entries (entries k * 128 to k * 128 + 127), lying in one group or among the device's own entries, and every neighbour group is named by some brick of every device. owner_cell[d, e] for e < 4096 is the cell of d's own entry e; for e >= 4096 it is the cell named by that entry of the device at d's position minus the step of group (e - 4096) // 512, or 4096 where that slot is empty. The used entries of one aligned window of 128 entries name cells of one aligned window of 128 cells.
All inputs are finite; a program needn't handle non-finite values.
Results may differ from a plain program's by a relative error of at most 0.017.
Values may be sent and summed in bfloat16 or wider, within the bound.
No kernel may reach another device: no remote copies, remote signals or barrier semaphores. Data moves between devices by JAX's collectives and lax.ppermute only.
A program may use at most 128 MiB of HBM per device.

v0:
```python
import functools

import jax
import jax.numpy as jnp
from jax import lax
from jax.experimental import pallas as pl
from jax.experimental.pallas import tpu as pltpu
from jax.sharding import PartitionSpec as P

BLK = 128
C_DEV = 4096
SELF_CAP = 4096
WIN = 128
BRICKS_PER_STEP = 32
UNROLL = 8
WIN_UNROLL = 4

step_table = ((-1, -1), (-1, 0), (-1, 1), (0, -1), (0, 1), (1, -1), (1, 0), (1, 1))

NT = (((1,), (1,)), ((), ()))
TN = (((0,), (0,)), ((), ()))


def split_parts(data):
    high = data.astype(jnp.bfloat16)
    low = (data - high.astype(jnp.float32)).astype(jnp.bfloat16)
    return high, low


def one_hot_rows(index_row):
    span = lax.broadcasted_iota(jnp.int32, (WIN, index_row.shape[1]), 0)
    return (span == index_row).astype(jnp.bfloat16)


def down_kernel(first_window, count_ref, order_ref, win_ref, off_ref, xt_ref, e_ref, w_ref, *refs):
    outs = refs[:-1]
    acc = refs[-1]
    step = pl.program_id(0)
    per_step = e_ref.shape[0]
    trash = acc.shape[0] // WIN - 1

    @pl.when(step == 0)
    def _():
        acc[...] = jnp.zeros_like(acc)

    neighbours = count_ref[step]
    if first_window == 0:
        start, stop = neighbours, per_step
    else:
        start, stop = 0, neighbours

    def body(u, carry):
        results = []
        for t in range(UNROLL):
            position = start + u * UNROLL + t
            j = order_ref[step * per_step + jnp.minimum(position, per_step - 1)]
            brick = step * per_step + j
            window = jnp.where(position < stop, win_ref[brick] - first_window, trash)
            offset = off_ref[brick]
            inside = jnp.bitwise_and(e_ref[pl.ds(j, 1), :], WIN - 1)
            pick = one_hot_rows(inside)
            cols = pl.ds(pl.multiple_of(j * BLK, BLK), BLK)
            summed = lax.dot_general(pick, xt_ref[:, cols], NT, preferred_element_type=jnp.float32)
            part = jnp.dot(summed.astype(jnp.bfloat16), w_ref[offset], preferred_element_type=jnp.float32)
            results.append((window, part))
        for window, part in results:
            rows = pl.ds(pl.multiple_of(window * WIN, WIN), WIN)
            acc[rows, :] += part
        return carry

    lax.fori_loop(0, (stop - start + UNROLL - 1) // UNROLL, body, 0)

    @pl.when(step == pl.num_programs(0) - 1)
    def _():
        size = outs[0].shape[0]
        for g, out in enumerate(outs):
            out[...] = acc[g * size : (g + 1) * size, :].astype(out.dtype)


def coarse_kernel(cw_ref, cells_ref, bias_ref, *refs):
    n_groups = len(step_table)
    sources = refs[: 1 + n_groups]
    outs = refs[1 + n_groups : 2 + 2 * n_groups]
    acc, coarse = refs[2 + 2 * n_groups :]
    cell_windows = acc.shape[0] // WIN
    acc[...] = jnp.zeros_like(acc)

    def pick_of(w):
        window = jnp.minimum(cw_ref[w], cell_windows - 1)
        cells = cells_ref[pl.ds(w, 1), :]
        inside = jnp.where(cells < C_DEV, cells - window * WIN, -1)
        rows = pl.ds(pl.multiple_of(window * WIN, WIN), WIN)
        return one_hot_rows(inside), rows

    base = 0
    for src in sources:
        count = src.shape[0] // WIN

        def gather_body(u, carry, src=src, base=base):
            results = []
            for t in range(WIN_UNROLL):
                j = u * WIN_UNROLL + t
                pick, rows = pick_of(base + j)
                entries = src[pl.ds(pl.multiple_of(j * WIN, WIN), WIN), :]
                results.append((rows, jnp.dot(pick, entries, preferred_element_type=jnp.float32)))
            for rows, value in results:
                acc[rows, :] += value
            return carry

        lax.fori_loop(0, count // WIN_UNROLL, gather_body, 0)
        base += count

    coarse[...] = jnp.maximum(acc[...] + bias_ref[...], 0.0).astype(jnp.bfloat16)

    base = 0
    for out in outs:
        count = out.shape[1] // WIN

        def scatter_body(u, carry, out=out, base=base):
            for t in range(WIN_UNROLL):
                j = u * WIN_UNROLL + t
                pick, rows = pick_of(base + j)
                chosen = lax.dot_general(coarse[rows, :], pick, TN, preferred_element_type=jnp.float32)
                out[:, pl.ds(pl.multiple_of(j * WIN, WIN), WIN)] = chosen.astype(jnp.bfloat16)
            return carry

        lax.fori_loop(0, count // WIN_UNROLL, scatter_body, 0)
        base += count


def up_kernel(own_mode, count_ref, order_ref, win_ref, off_ref, xt_ref, e_ref, wt_ref, *refs):
    step = pl.program_id(0)
    per_step = e_ref.shape[0]
    neighbours = count_ref[step]
    if own_mode:
        parents_ref, out_ref = refs
        first_window = 0
        start, stop = neighbours, per_step
    else:
        n_groups = len(step_table)
        sources = refs[:n_groups]
        prev_ref, out_ref, parents_ref, sems = refs[n_groups:]
        first_window = SELF_CAP // WIN
        start, stop = 0, neighbours

        @pl.when(step == 0)
        def _():
            copies = []
            offset = 0
            for index, src in enumerate(sources):
                size = src.shape[1]
                copy = pltpu.make_async_copy(src, parents_ref.at[:, pl.ds(offset, size)], sems.at[index])
                copy.start()
                copies.append(copy)
                offset += size
            for copy in copies:
                copy.wait()

        out_ref[...] = prev_ref[...]

    def body(u, carry):
        for t in range(UNROLL):
            position = jnp.minimum(start + u * UNROLL + t, stop - 1)
            j = order_ref[step * per_step + position]
            brick = step * per_step + j
            window = win_ref[brick] - first_window
            offset = off_ref[brick]
            inside = jnp.bitwise_and(e_ref[pl.ds(j, 1), :], WIN - 1)
            pick = one_hot_rows(inside)
            parents = parents_ref[:, pl.ds(pl.multiple_of(window * WIN, WIN), WIN)]
            rows_t = jnp.dot(parents, pick, preferred_element_type=jnp.float32).astype(jnp.bfloat16)
            lifted = jnp.dot(wt_ref[offset], rows_t, preferred_element_type=jnp.float32)
            cols = pl.ds(pl.multiple_of(j * BLK, BLK), BLK)
            out_ref[:, cols] = (xt_ref[:, cols].astype(jnp.float32) + lifted).astype(out_ref.dtype)
        return carry

    lax.fori_loop(0, (stop - start + UNROLL - 1) // UNROLL, body, 0)


def group_route(g, sign):
    n_outer = lax.axis_size("outer")
    n_inner = lax.axis_size("inner")
    a, b = step_table[g]
    route = []
    for s in range(n_outer * n_inner):
        row, col = divmod(s, n_inner)
        owner = ((row + a) % n_outer) * n_inner + (col + b) % n_inner
        route.append((s, owner) if sign > 0 else (owner, s))
    return route


def local(features, block_offset, parent_entry, owner_cell, w_down, b_down, w_up):
    n_groups = len(step_table)
    fine_rows, in_width = features.shape
    out_width = w_down.shape[2]
    entries = owner_cell.shape[1]
    cap = (entries - SELF_CAP) // n_groups
    blocks = fine_rows // BLK
    steps = blocks // BRICKS_PER_STEP

    xt = features.T
    entry_rows = parent_entry.reshape(blocks, BLK)
    brick_window = entry_rows[:, 0] // WIN
    cells = owner_cell.reshape(entries // WIN, WIN)
    cell_window = jnp.min(cells, axis=1) // WIN
    w_up_t = jnp.swapaxes(w_up, 1, 2)

    part_shapes = [jax.ShapeDtypeStruct((SELF_CAP, out_width), jnp.bfloat16)] + [
        jax.ShapeDtypeStruct((cap, out_width), jnp.bfloat16)
    ] * n_groups
    answer_shapes = [jax.ShapeDtypeStruct((s.shape[1], s.shape[0]), s.dtype) for s in part_shapes]
    whole = lambda shape: pl.BlockSpec(shape, lambda *idx: (0,) * len(shape))

    is_far = (brick_window >= SELF_CAP // WIN).astype(jnp.int32).reshape(steps, BRICKS_PER_STEP)
    far_count = jnp.sum(is_far, axis=1)
    far_rank = jnp.cumsum(is_far, axis=1) - is_far
    own_rank = jnp.cumsum(1 - is_far, axis=1) - (1 - is_far)
    position = jnp.where(is_far == 1, far_rank, far_count[:, None] + own_rank)
    local_ids = jnp.arange(BRICKS_PER_STEP, dtype=jnp.int32)
    order = jnp.sum(
        jnp.where(position[:, None, :] == local_ids[None, :, None], local_ids[None, None, :], 0), axis=2
    )
    order = order.reshape(blocks).astype(jnp.int32)
    counts = far_count.astype(jnp.int32)

    def down_call(first_window, shapes):
        rows = sum(s.shape[0] for s in shapes)
        return pl.pallas_call(
            functools.partial(down_kernel, first_window),
            out_shape=shapes,
            grid_spec=pltpu.PrefetchScalarGridSpec(
                num_scalar_prefetch=4,
                grid=(steps,),
                in_specs=[
                    pl.BlockSpec((in_width, BRICKS_PER_STEP * BLK), lambda i, *_: (0, i)),
                    pl.BlockSpec((BRICKS_PER_STEP, BLK), lambda i, *_: (i, 0)),
                    whole(w_down.shape),
                ],
                out_specs=[whole(s.shape) for s in shapes],
                scratch_shapes=[pltpu.VMEM((rows + WIN, out_width), jnp.float32)],
            ),
            compiler_params=pltpu.CompilerParams(dimension_semantics=("arbitrary",)),
            cost_estimate=pl.CostEstimate(
                flops=2 * fine_rows * in_width * out_width,
                transcendentals=0,
                bytes_accessed=fine_rows * (in_width * 2 + 4) + rows * out_width * 2,
            ),
        )(counts, order, brick_window, block_offset, xt, entry_rows, w_down)

    parts = [None] + list(down_call(SELF_CAP // WIN, part_shapes[1:]))
    parts[0] = down_call(0, part_shapes[:1])[0]

    arrived = [
        lax.ppermute(parts[1 + g], ("outer", "inner"), group_route(g, 1)) for g in range(n_groups)
    ]

    coarse = pl.pallas_call(
        coarse_kernel,
        out_shape=answer_shapes,
        grid_spec=pltpu.PrefetchScalarGridSpec(
            num_scalar_prefetch=1,
            grid=(1,),
            in_specs=[whole(cells.shape), whole((1, out_width))]
            + [whole(s.shape) for s in part_shapes],
            out_specs=[whole(s.shape) for s in answer_shapes],
            scratch_shapes=[
                pltpu.VMEM((C_DEV, out_width), jnp.float32),
                pltpu.VMEM((C_DEV, out_width), jnp.bfloat16),
            ],
        ),
        cost_estimate=pl.CostEstimate(
            flops=4 * entries * WIN * out_width,
            transcendentals=0,
            bytes_accessed=4 * entries * out_width,
        ),
    )
    answers = coarse(cell_window, cells, b_down.reshape(1, out_width), parts[0], *arrived)

    returned = [
        lax.ppermute(answers[1 + g], ("outer", "inner"), group_route(g, -1)) for g in range(n_groups)
    ]

    chunk = pl.BlockSpec((in_width, BRICKS_PER_STEP * BLK), lambda i, *_: (0, i))
    rows_spec = pl.BlockSpec((BRICKS_PER_STEP, BLK), lambda i, *_: (i, 0))
    out_shape = jax.ShapeDtypeStruct((in_width, fine_rows), features.dtype)
    up_cost = pl.CostEstimate(
        flops=2 * fine_rows * in_width * out_width,
        transcendentals=0,
        bytes_accessed=fine_rows * (in_width * 2 + 2),
    )
    own_up = pl.pallas_call(
        functools.partial(up_kernel, True),
        out_shape=out_shape,
        grid_spec=pltpu.PrefetchScalarGridSpec(
            num_scalar_prefetch=4,
            grid=(steps,),
            in_specs=[chunk, rows_spec, whole(w_up_t.shape), whole(answer_shapes[0].shape)],
            out_specs=chunk,
        ),
        compiler_params=pltpu.CompilerParams(dimension_semantics=("arbitrary",)),
        cost_estimate=up_cost,
    )
    partial_out = own_up(counts, order, brick_window, block_offset, xt, entry_rows, w_up_t, answers[0])

    far_up = pl.pallas_call(
        functools.partial(up_kernel, False),
        out_shape=out_shape,
        grid_spec=pltpu.PrefetchScalarGridSpec(
            num_scalar_prefetch=4,
            grid=(steps,),
            in_specs=[chunk, rows_spec, whole(w_up_t.shape)]
            + [pl.BlockSpec(memory_space=pl.ANY)] * n_groups
            + [chunk],
            out_specs=chunk,
            scratch_shapes=[
                pltpu.VMEM((out_width, entries - SELF_CAP), jnp.bfloat16),
                pltpu.SemaphoreType.DMA((n_groups,)),
            ],
        ),
        input_output_aliases={4 + 3 + n_groups: 0},
        compiler_params=pltpu.CompilerParams(dimension_semantics=("arbitrary",)),
        cost_estimate=up_cost,
    )
    out_t = far_up(counts, order, brick_window, block_offset, xt, entry_rows, w_up_t, *returned, partial_out)
    return out_t.T


def solution(mesh):
    in_specs = (
        P(("outer", "inner"), None),
        P(("outer", "inner")),
        P(("outer", "inner")),
        P(("outer", "inner"), None),
        P(),
        P(),
        P(),
    )
    out_specs = P(("outer", "inner"), None)
    return jax.shard_map(local, mesh=mesh, in_specs=in_specs, out_specs=out_specs, check_vma=False)
```

profile of v0, /device:TPU:24, one launch (start us, length us, event | category | flops | bytes accessed | tf_op | source)
XLA Modules:
  0.0 101.4 jit_solution(1810812653545371701)
XLA Ops:
  0.0 1.0 slice_reduce_fusion
  1.0 0.6 and_select_fusion.1.win_ref
  1.6 0.1 squeeze.5
  1.7 0.1 convert_reduce_fusion.count_ref
  1.9 0.2 reduce_window_sum.18
  2.0 0.2 reduce_window_sum.17
  2.2 0.1 fusion.2
  2.3 0.2 select_reduce_fusion
  2.5 0.7 reshape.112.order_ref
  3.2 13.1 %shard_map.74 = (bf16[512,128]{1,0:T(8,128)(2,1)}, bf16[512,128]{1,0:T(8,128)(2,1)}, bf16[512,128]{1,0:T(8,128)(2,1)}, bf16[512,128]{1,0:T(8,128)(2,1)}, bf16[51...) custom-call(s32[8]{0:T(128)} %copy-done.17, ...), custom_call_target="tpu_custom_call" | custom-call | flops 536870912 | bytes 5373952 | tf_op jit(solution)/shard_map/pallas_call | solution.py:228
  16.3 6.4 %collective-permute-start = (bf16[512,128]{1,0:T(8,128)(2,1)}, bf16[512,128]{1,0:T(8,128)(2,1)S(1)}, u32[]{:S(2)}, u32[]{:S(2)}) collective-permute-start(bf16[512,128]{1,0:T(8,128)(2,1)} %get-tuple-element.22), channel_id=1, source_target_pairs={{0,127},{1,120},{2,121},{3,122},{4,123},{5,124},{6,125},{7,126},{8... | collective-permute-start | bytes 393224 | tf_op jit(solution)/shard_map/ppermute | solution.py:254
  22.7 0.8 collective-permute-start.1
  23.5 1.9 %collective-permute-start.2 = (bf16[512,128]{1,0:T(8,128)(2,1)}, bf16[512,128]{1,0:T(8,128)(2,1)S(1)}, u32[]{:S(2)}, u32[]{:S(2)}) collective-permute-start(bf16[512,128]{1,0:T(8,128)(2,1)} %get-tuple-element.24), channel_id=1, source_target_pairs={{0,121},{1,122},{2,123},{3,124},{4,125},{5,126},{6,127},{7,120},{8... | collective-permute-start | bytes 393224 | tf_op jit(solution)/shard_map/ppermute | solution.py:254
  25.4 1.3 %collective-permute-start.3 = (bf16[512,128]{1,0:T(8,128)(2,1)}, bf16[512,128]{1,0:T(8,128)(2,1)S(1)}, u32[]{:S(2)}, u32[]{:S(2)}) collective-permute-start(bf16[512,128]{1,0:T(8,128)(2,1)} %get-tuple-element.25), channel_id=1, source_target_pairs={{0,7},{1,0},{2,1},{3,2},{4,3},{5,4},{6,5},{7,6},{8,15},{9,8},{10,9... | collective-permute-start | bytes 393224 | tf_op jit(solution)/shard_map/ppermute | solution.py:254
  26.6 0.0 collective-permute-start.4
  26.6 0.0 copy-done.8
  26.6 0.1 reduce_min.9
  26.8 0.1 collective-permute-done.refs_1_
  26.9 1.4 %collective-permute-start.5 = (bf16[512,128]{1,0:T(8,128)(2,1)}, bf16[512,128]{1,0:T(8,128)(2,1)S(1)}, u32[]{:S(2)}, u32[]{:S(2)}) collective-permute-start(bf16[512,128]{1,0:T(8,128)(2,1)} %get-tuple-element.27), channel_id=1, source_target_pairs={{0,15},{1,8},{2,9},{3,10},{4,11},{5,12},{6,13},{7,14},{8,23},{9,16... | collective-permute-start | bytes 393224 | tf_op jit(solution)/shard_map/ppermute | solution.py:254
  28.2 1.5 %collective-permute-done.1.refs_2_ = bf16[512,128]{1,0:T(8,128)(2,1)S(1)} collective-permute-done((bf16[512,128]{1,0:T(8,128)(2,1)}, bf16[512,128]{1,0:T(8,128)(2,1)S(1)}, u32[]{:S(2)}, u32[]{:S(2)}) %collective-permute-start.1) | collective-permute-done | bytes 131104 | tf_op jit(solution)/shard_map/ppermute | solution.py:254
  29.7 0.0 collective-permute-start.6
  29.7 2.6 %collective-permute-done.2.refs_3_ = bf16[512,128]{1,0:T(8,128)(2,1)S(1)} collective-permute-done((bf16[512,128]{1,0:T(8,128)(2,1)}, bf16[512,128]{1,0:T(8,128)(2,1)S(1)}, u32[]{:S(2)}, u32[]{:S(2)}) %collective-permute-start.2) | collective-permute-done | bytes 131104 | tf_op jit(solution)/shard_map/ppermute | solution.py:254
  32.4 0.0 collective-permute-start.7
  32.4 0.6 and_select_fusion.cw_ref
  32.9 13.0 %shard_map.73.refs_0_ = bf16[4096,128]{1,0:T(8,128)(2,1)} custom-call(s32[8]{0:T(128)} %copy-done.17, s32[256]{0:T(256)} %reshape.112.order_ref, s32[256]{0:T(256)} %and_select_fusion.1.win_ref, s32[256]{0:T(256)} %off_ref.7, bf16[64,32768]{1,0:T(8,128)(2,1)} %bitcast.7, s32[256,128]{1,0:T(8,128)} %bitcast.12, bf16[8,64,128]{2,1,0:T(8,128)(2,1)} %w_ref.3), custom_call_target="tpu_custom_call" | custom-call | flops 536870912 | bytes 5373952 | tf_op jit(solution)/shard_map/pallas_call | solution.py:228
  46.0 0.0 collective-permute-done.3.refs_4_
  46.0 0.0 collective-permute-done.4.refs_5_
  46.0 0.0 copy-start.13
  46.0 0.0 collective-permute-done.5.refs_6_
  46.0 0.0 collective-permute-done.6.refs_7_
  46.0 0.0 collective-permute-done.7.refs_8_
  46.0 0.0 copy-start.16
  46.0 0.0 copy-done.9
  46.1 0.0 copy-done.10
  46.1 0.0 copy-done.11
  46.1 0.5 copy-done.12
  46.6 0.1 copy-done.13
  46.7 0.1 copy-done.14
  46.7 0.0 copy-done.15
  46.8 0.0 copy-done.16
  46.8 8.0 %shard_map.75 = (bf16[128,4096]{1,0:T(8,128)(2,1)}, bf16[128,512]{1,0:T(8,128)(2,1)}, bf16[128,512]{1,0:T(8,128)(2,1)}, bf16[128,512]{1,0:T(8,128)(2,1)}, bf16[1...) custom-call(s32[64]{0:T(128)} %and_select_fusion.cw_ref, ...), custom_call_target="tpu_custom_call" | custom-call | flops 536870912 | bytes 4194304 | tf_op jit(solution)/shard_map/pallas_call | solution.py:277
  54.8 2.2 %collective-permute-start.8 = (bf16[128,512]{1,0:T(8,128)(2,1)}, bf16[128,512]{1,0:T(8,128)(2,1)S(1)}, u32[]{:S(2)}, u32[]{:S(2)}) collective-permute-start(bf16[128,512]{1,0:T(8,128)(2,1)} %get-tuple-element.30), channel_id=1, source_target_pairs={{127,0},{120,1},{121,2},{122,3},{123,4},{124,5},{125,6},{126,7},{7... | collective-permute-start | bytes 393224 | tf_op jit(solution)/shard_map/ppermute | solution.py:280
  57.0 2.1 %collective-permute-start.9 = (bf16[128,512]{1,0:T(8,128)(2,1)}, bf16[128,512]{1,0:T(8,128)(2,1)S(1)}, u32[]{:S(2)}, u32[]{:S(2)}) collective-permute-start(bf16[128,512]{1,0:T(8,128)(2,1)} %get-tuple-element.31), channel_id=1, source_target_pairs={{120,0},{121,1},{122,2},{123,3},{124,4},{125,5},{126,6},{127,7},{0... | collective-permute-start | bytes 393224 | tf_op jit(solution)/shard_map/ppermute | solution.py:280
  59.1 0.0 collective-permute-start.10
  59.1 0.1 collective-permute-start.11
  59.3 1.6 %collective-permute-start.12 = (bf16[128,512]{1,0:T(8,128)(2,1)}, bf16[128,512]{1,0:T(8,128)(2,1)S(1)}, u32[]{:S(2)}, u32[]{:S(2)}) collective-permute-start(bf16[128,512]{1,0:T(8,128)(2,1)} %get-tuple-element.34), channel_id=1, source_target_pairs={{1,0},{2,1},{3,2},{4,3},{5,4},{6,5},{7,6},{0,7},{9,8},{10,9},{11,1... | collective-permute-start | bytes 393224 | tf_op jit(solution)/shard_map/ppermute | solution.py:280
  60.9 3.6 %collective-permute-done.8.refs_0_ = bf16[128,512]{1,0:T(8,128)(2,1)S(1)} collective-permute-done((bf16[128,512]{1,0:T(8,128)(2,1)}, bf16[128,512]{1,0:T(8,128)(2,1)S(1)}, u32[]{:S(2)}, u32[]{:S(2)}) %collective-permute-start.8) | collective-permute-done | bytes 131104 | tf_op jit(solution)/shard_map/ppermute | solution.py:280
  64.5 3.2 %collective-permute-start.13 = (bf16[128,512]{1,0:T(8,128)(2,1)}, bf16[128,512]{1,0:T(8,128)(2,1)S(1)}, u32[]{:S(2)}, u32[]{:S(2)}) collective-permute-start(bf16[128,512]{1,0:T(8,128)(2,1)} %get-tuple-element.35), channel_id=1, source_target_pairs={{15,0},{8,1},{9,2},{10,3},{11,4},{12,5},{13,6},{14,7},{23,8},{16,9... | collective-permute-start | bytes 393224 | tf_op jit(solution)/shard_map/ppermute | solution.py:280
  67.6 0.6 collective-permute-done.9.refs_1_
  68.3 2.6 %collective-permute-start.14 = (bf16[128,512]{1,0:T(8,128)(2,1)}, bf16[128,512]{1,0:T(8,128)(2,1)S(1)}, u32[]{:S(2)}, u32[]{:S(2)}) collective-permute-start(bf16[128,512]{1,0:T(8,128)(2,1)} %get-tuple-element.36), channel_id=1, source_target_pairs={{8,0},{9,1},{10,2},{11,3},{12,4},{13,5},{14,6},{15,7},{16,8},{17,9... | collective-permute-start | bytes 393224 | tf_op jit(solution)/shard_map/ppermute | solution.py:280
  70.9 0.5 collective-permute-done.10.refs_2_
  71.4 2.4 %collective-permute-start.15 = (bf16[128,512]{1,0:T(8,128)(2,1)}, bf16[128,512]{1,0:T(8,128)(2,1)S(1)}, u32[]{:S(2)}, u32[]{:S(2)}) collective-permute-start(bf16[128,512]{1,0:T(8,128)(2,1)} %get-tuple-element.37), channel_id=1, source_target_pairs={{9,0},{10,1},{11,2},{12,3},{13,4},{14,5},{15,6},{8,7},{17,8},{18,9... | collective-permute-start | bytes 393224 | tf_op jit(solution)/shard_map/ppermute | solution.py:280
  73.9 12.0 %shard_map.76.refs_8_ = bf16[64,32768]{1,0:T(8,128)(2,1)} custom-call(s32[8]{0:T(128)} %copy-done.17, s32[256]{0:T(256)} %reshape.112.order_ref, s32[256]{0:T(256)} %and_select_fusion.1.win_ref, s32[256]{0:T(256)} %off_ref.7, bf16[64,32768]{1,0:T(8,128)(2,1)} %bitcast.8, s32[256,128]{1,0:T(8,128)} %bitcast.13, bf16[8,64,128]{2,1,0:T(8,128)(2,1)} %bitcast.15, ...), custom_call_target="tpu_custom_call" | custom-call | flops 536870912 | bytes 4259840 | tf_op jit(solution)/shard_map/pallas_call | solution.py:303
  85.9 0.0 collective-permute-done.11.refs_3_
  85.9 0.0 collective-permute-done.12.refs_4_
  86.0 0.0 collective-permute-done.13.refs_5_
  86.0 0.0 collective-permute-done.14.refs_6_
  86.0 0.0 collective-permute-done.15.refs_7_
  86.0 0.6 copy-done.3
  86.6 0.1 copy-done.4
  86.6 0.1 copy-done.5
  86.7 0.0 copy-done.6
  86.7 0.6 copy-done.7
  87.4 14.0 %shard_map.77 = bf16[64,32768]{1,0:T(8,128)(2,1)} custom-call(s32[8]{0:T(128)} %copy-done.17, s32[256]{0:T(256)} %reshape.112.order_ref, s32[256]{0:T(256)} %and_select_fusion.1.win_ref, s32[256]{0:T(256)} %off_ref.7, bf16[64,32768]{1,0:T(8,128)(2,1)} %bitcast.9, s32[256,128]{1,0:T(8,128)} %bitcast.14, ...), custom_call_target="tpu_custom_call", output_to_operand_aliasing={{}: (15, {})} | custom-call | flops 536870912 | bytes 4259840 | tf_op jit(solution)/shard_map/pallas_call | solution.py:324
  (22 shorter events, 0.1 us)
Async XLA Ops:
  0.0 26.6 %copy-start.8 = (s32[1,8192]{1,0:T(1,128)S(1)}, s32[1,8192]{1,0:T(1,128)}, u32[]{:S(2)}) copy-start(s32[1,8192]{1,0:T(1,128)} %param.10) | copy-start | bytes 98308
  1.8 1.3 %copy-start.17 = (s32[8]{0:T(128)}, s32[8]{0:T(128)S(1)}, u32[]{:S(2)}) copy-start(s32[8]{0:T(128)S(1)} %convert_reduce_fusion.count_ref) | copy-start | bytes 100
  16.3 10.6 %collective-permute-start = (bf16[512,128]{1,0:T(8,128)(2,1)}, bf16[512,128]{1,0:T(8,128)(2,1)S(1)}, u32[]{:S(2)}, u32[]{:S(2)}) collective-permute-start(bf16[512,128]{1,0:T(8,128)(2,1)} %get-tuple-element.22), channel_id=1, source_target_pairs={{0,127},{1,120},{2,121},{3,122},{4,123},{5,124},{6,125},{7,126},{8... | collective-permute-start | bytes 393224 | tf_op jit(solution)/shard_map/ppermute | solution.py:254
  22.7 7.1 %collective-permute-start.1 = (bf16[512,128]{1,0:T(8,128)(2,1)}, bf16[512,128]{1,0:T(8,128)(2,1)S(1)}, u32[]{:S(2)}, u32[]{:S(2)}) collective-permute-start(bf16[512,128]{1,0:T(8,128)(2,1)} %get-tuple-element.23), channel_id=1, source_target_pairs={{0,120},{1,121},{2,122},{3,123},{4,124},{5,125},{6,126},{7,127},{8... | collective-permute-start | bytes 393224 | tf_op jit(solution)/shard_map/ppermute | solution.py:254
  23.5 8.9 %collective-permute-start.2 = (bf16[512,128]{1,0:T(8,128)(2,1)}, bf16[512,128]{1,0:T(8,128)(2,1)S(1)}, u32[]{:S(2)}, u32[]{:S(2)}) collective-permute-start(bf16[512,128]{1,0:T(8,128)(2,1)} %get-tuple-element.24), channel_id=1, source_target_pairs={{0,121},{1,122},{2,123},{3,124},{4,125},{5,126},{6,127},{7,120},{8... | collective-permute-start | bytes 393224 | tf_op jit(solution)/shard_map/ppermute | solution.py:254
  25.4 20.6 %collective-permute-start.3 = (bf16[512,128]{1,0:T(8,128)(2,1)}, bf16[512,128]{1,0:T(8,128)(2,1)S(1)}, u32[]{:S(2)}, u32[]{:S(2)}) collective-permute-start(bf16[512,128]{1,0:T(8,128)(2,1)} %get-tuple-element.25), channel_id=1, source_target_pairs={{0,7},{1,0},{2,1},{3,2},{4,3},{5,4},{6,5},{7,6},{8,15},{9,8},{10,9... | collective-permute-start | bytes 393224 | tf_op jit(solution)/shard_map/ppermute | solution.py:254
  26.6 19.3 %collective-permute-start.4 = (bf16[512,128]{1,0:T(8,128)(2,1)}, bf16[512,128]{1,0:T(8,128)(2,1)S(1)}, u32[]{:S(2)}, u32[]{:S(2)}) collective-permute-start(bf16[512,128]{1,0:T(8,128)(2,1)} %get-tuple-element.26), channel_id=1, source_target_pairs={{0,1},{1,2},{2,3},{3,4},{4,5},{5,6},{6,7},{7,0},{8,9},{9,10},{10,1... | collective-permute-start | bytes 393224 | tf_op jit(solution)/shard_map/ppermute | solution.py:254
  26.9 19.2 %copy-start.9 = (bf16[512,128]{1,0:T(8,128)(2,1)}, bf16[512,128]{1,0:T(8,128)(2,1)S(1)}, u32[]{:S(2)}) copy-start(bf16[512,128]{1,0:T(8,128)(2,1)S(1)} %collective-permute-done.refs_1_) | copy-start | bytes 393220
  26.9 19.1 %collective-permute-start.5 = (bf16[512,128]{1,0:T(8,128)(2,1)}, bf16[512,128]{1,0:T(8,128)(2,1)S(1)}, u32[]{:S(2)}, u32[]{:S(2)}) collective-permute-start(bf16[512,128]{1,0:T(8,128)(2,1)} %get-tuple-element.27), channel_id=1, source_target_pairs={{0,15},{1,8},{2,9},{3,10},{4,11},{5,12},{6,13},{7,14},{8,23},{9,16... | collective-permute-start | bytes 393224 | tf_op jit(solution)/shard_map/ppermute | solution.py:254
  29.7 16.3 %copy-start.10 = (bf16[512,128]{1,0:T(8,128)(2,1)}, bf16[512,128]{1,0:T(8,128)(2,1)S(1)}, u32[]{:S(2)}) copy-start(bf16[512,128]{1,0:T(8,128)(2,1)S(1)} %collective-permute-done.1.refs_2_) | copy-start | bytes 393220
  29.7 16.3 %collective-permute-start.6 = (bf16[512,128]{1,0:T(8,128)(2,1)}, bf16[512,128]{1,0:T(8,128)(2,1)S(1)}, u32[]{:S(2)}, u32[]{:S(2)}) collective-permute-start(bf16[512,128]{1,0:T(8,128)(2,1)} %get-tuple-element.28), channel_id=1, source_target_pairs={{0,8},{1,9},{2,10},{3,11},{4,12},{5,13},{6,14},{7,15},{8,16},{9,17... | collective-permute-start | bytes 393224 | tf_op jit(solution)/shard_map/ppermute | solution.py:254
  32.3 13.7 %copy-start.11 = (bf16[512,128]{1,0:T(8,128)(2,1)}, bf16[512,128]{1,0:T(8,128)(2,1)S(1)}, u32[]{:S(2)}) copy-start(bf16[512,128]{1,0:T(8,128)(2,1)S(1)} %collective-permute-done.2.refs_3_) | copy-start | bytes 393220
  32.4 13.7 %collective-permute-start.7 = (bf16[512,128]{1,0:T(8,128)(2,1)}, bf16[512,128]{1,0:T(8,128)(2,1)S(1)}, u32[]{:S(2)}, u32[]{:S(2)}) collective-permute-start(bf16[512,128]{1,0:T(8,128)(2,1)} %get-tuple-element.29), channel_id=1, source_target_pairs={{0,9},{1,10},{2,11},{3,12},{4,13},{5,14},{6,15},{7,8},{8,17},{9,18... | collective-permute-start | bytes 393224 | tf_op jit(solution)/shard_map/ppermute | solution.py:254
  46.0 0.6 copy-start.12
  46.0 0.7 copy-start.13
  46.0 0.7 copy-start.14
  46.0 0.8 copy-start.15
  46.0 0.8 copy-start.16
  54.8 9.6 %collective-permute-start.8 = (bf16[128,512]{1,0:T(8,128)(2,1)}, bf16[128,512]{1,0:T(8,128)(2,1)S(1)}, u32[]{:S(2)}, u32[]{:S(2)}) collective-permute-start(bf16[128,512]{1,0:T(8,128)(2,1)} %get-tuple-element.30), channel_id=1, source_target_pairs={{127,0},{120,1},{121,2},{122,3},{123,4},{124,5},{125,6},{126,7},{7... | collective-permute-start | bytes 393224 | tf_op jit(solution)/shard_map/ppermute | solution.py:280
  57.0 11.3 %collective-permute-start.9 = (bf16[128,512]{1,0:T(8,128)(2,1)}, bf16[128,512]{1,0:T(8,128)(2,1)S(1)}, u32[]{:S(2)}, u32[]{:S(2)}) collective-permute-start(bf16[128,512]{1,0:T(8,128)(2,1)} %get-tuple-element.31), channel_id=1, source_target_pairs={{120,0},{121,1},{122,2},{123,3},{124,4},{125,5},{126,6},{127,7},{0... | collective-permute-start | bytes 393224 | tf_op jit(solution)/shard_map/ppermute | solution.py:280
  59.1 12.3 %collective-permute-start.10 = (bf16[128,512]{1,0:T(8,128)(2,1)}, bf16[128,512]{1,0:T(8,128)(2,1)S(1)}, u32[]{:S(2)}, u32[]{:S(2)}) collective-permute-start(bf16[128,512]{1,0:T(8,128)(2,1)} %get-tuple-element.32), channel_id=1, source_target_pairs={{121,0},{122,1},{123,2},{124,3},{125,4},{126,5},{127,6},{120,7},{1... | collective-permute-start | bytes 393224 | tf_op jit(solution)/shard_map/ppermute | solution.py:280
  59.1 26.8 %collective-permute-start.11 = (bf16[128,512]{1,0:T(8,128)(2,1)}, bf16[128,512]{1,0:T(8,128)(2,1)S(1)}, u32[]{:S(2)}, u32[]{:S(2)}) collective-permute-start(bf16[128,512]{1,0:T(8,128)(2,1)} %get-tuple-element.33), channel_id=1, source_target_pairs={{7,0},{0,1},{1,2},{2,3},{3,4},{4,5},{5,6},{6,7},{15,8},{8,9},{9,10... | collective-permute-start | bytes 393224 | tf_op jit(solution)/shard_map/ppermute | solution.py:280
  59.3 26.7 %collective-permute-start.12 = (bf16[128,512]{1,0:T(8,128)(2,1)}, bf16[128,512]{1,0:T(8,128)(2,1)S(1)}, u32[]{:S(2)}, u32[]{:S(2)}) collective-permute-start(bf16[128,512]{1,0:T(8,128)(2,1)} %get-tuple-element.34), channel_id=1, source_target_pairs={{1,0},{2,1},{3,2},{4,3},{5,4},{6,5},{7,6},{0,7},{9,8},{10,9},{11,1... | collective-permute-start | bytes 393224 | tf_op jit(solution)/shard_map/ppermute | solution.py:280
  64.4 21.5 %copy-start = (bf16[128,512]{1,0:T(8,128)(2,1)}, bf16[128,512]{1,0:T(8,128)(2,1)S(1)}, u32[]{:S(2)}) copy-start(bf16[128,512]{1,0:T(8,128)(2,1)S(1)} %collective-permute-done.8.refs_0_) | copy-start | bytes 393220
  64.5 21.5 %collective-permute-start.13 = (bf16[128,512]{1,0:T(8,128)(2,1)}, bf16[128,512]{1,0:T(8,128)(2,1)S(1)}, u32[]{:S(2)}, u32[]{:S(2)}) collective-permute-start(bf16[128,512]{1,0:T(8,128)(2,1)} %get-tuple-element.35), channel_id=1, source_target_pairs={{15,0},{8,1},{9,2},{10,3},{11,4},{12,5},{13,6},{14,7},{23,8},{16,9... | collective-permute-start | bytes 393224 | tf_op jit(solution)/shard_map/ppermute | solution.py:280
  68.3 17.6 %copy-start.1 = (bf16[128,512]{1,0:T(8,128)(2,1)}, bf16[128,512]{1,0:T(8,128)(2,1)S(1)}, u32[]{:S(2)}) copy-start(bf16[128,512]{1,0:T(8,128)(2,1)S(1)} %collective-permute-done.9.refs_1_) | copy-start | bytes 393220
  68.3 17.7 %collective-permute-start.14 = (bf16[128,512]{1,0:T(8,128)(2,1)}, bf16[128,512]{1,0:T(8,128)(2,1)S(1)}, u32[]{:S(2)}, u32[]{:S(2)}) collective-permute-start(bf16[128,512]{1,0:T(8,128)(2,1)} %get-tuple-element.36), channel_id=1, source_target_pairs={{8,0},{9,1},{10,2},{11,3},{12,4},{13,5},{14,6},{15,7},{16,8},{17,9... | collective-permute-start | bytes 393224 | tf_op jit(solution)/shard_map/ppermute | solution.py:280
  71.4 14.5 %copy-start.2 = (bf16[128,512]{1,0:T(8,128)(2,1)}, bf16[128,512]{1,0:T(8,128)(2,1)S(1)}, u32[]{:S(2)}) copy-start(bf16[128,512]{1,0:T(8,128)(2,1)S(1)} %collective-permute-done.10.refs_2_) | copy-start | bytes 393220
  71.4 14.6 %collective-permute-start.15 = (bf16[128,512]{1,0:T(8,128)(2,1)}, bf16[128,512]{1,0:T(8,128)(2,1)S(1)}, u32[]{:S(2)}, u32[]{:S(2)}) collective-permute-start(bf16[128,512]{1,0:T(8,128)(2,1)} %get-tuple-element.37), channel_id=1, source_target_pairs={{9,0},{10,1},{11,2},{12,3},{13,4},{14,5},{15,6},{8,7},{17,8},{18,9... | collective-permute-start | bytes 393224 | tf_op jit(solution)/shard_map/ppermute | solution.py:280
  85.9 0.6 copy-start.3
  86.0 0.7 copy-start.4
  86.0 0.7 copy-start.5
  86.0 0.7 copy-start.6
  86.7 0.6 copy-start.7
where the time goes:
time: 103 us; the launch traced here: 101 us
  Pallas kernels  60.2 us (58%)
  starting transfers between devices  26 us (25%)
  waiting for transfers between devices  8.98 us (9%)
  local copies, waits for them, and re-layouts  3.91 us (4%)
  other arithmetic  2.07 us (2%)
    pallas_call x2, Pallas kernels, down_call(): pl.pallas_call(functools.partial(down_kernel, first_window), out_shape=sh...  26.2 us
    ppermute x8, starting transfers between devices, local(): lax.ppermute(answers[1 + g], ('outer', 'inner'), group_route(g, -1))  14.3 us
    pallas_call x1, Pallas kernels, local(): far_up(counts, order, brick_window, block_offset, xt, entry_rows, w_up_t,...  14 us
    pallas_call x1, Pallas kernels, local(): own_up(counts, order, brick_window, block_offset, xt, entry_rows, w_up_t,...  12 us
    ppermute x8, starting transfers between devices, local(): lax.ppermute(parts[1 + g], ('outer', 'inner'), group_route(g, 1))  11.7 us
    pallas_call x1, Pallas kernels, local(): coarse(cell_window, cells, b_down.reshape(1, out_width), parts[0], *arrived)  8 us
    ppermute x8, waiting for transfers between devices, local(): lax.ppermute(answers[1 + g], ('outer', 'inner'), group_route(g, -1))  4.77 us
    ppermute x8, waiting for transfers between devices, local(): lax.ppermute(parts[1 + g], ('outer', 'inner'), group_route(g, 1))  4.21 us
  transfers between devices with their start and end apart: 16, of which 6 were waited for; matrix products, arithmetic and copies ran while one was open for 1% of the time, Pallas kernels for 25%

commit v1 on v0

--- a/solution.py
+++ b/solution.py
@@ -11,9 +11,10 @@
 C_DEV = 4096
 SELF_CAP = 4096
 WIN = 128
-BRICKS_PER_STEP = 32
-UNROLL = 8
-WIN_UNROLL = 4
+BRICKS_PER_STEP = 64
+UNROLL = 16
+SPLIT_UNROLL = 16
+WIN_UNROLL = 16
 
 step_table = ((-1, -1), (-1, 0), (-1, 1), (0, -1), (0, 1), (1, -1), (1, 0), (1, 1))
 
@@ -49,26 +50,29 @@
     else:
         start, stop = 0, neighbours
 
-    def body(u, carry):
-        results = []
-        for t in range(UNROLL):
-            position = start + u * UNROLL + t
-            j = order_ref[step * per_step + jnp.minimum(position, per_step - 1)]
-            brick = step * per_step + j
-            window = jnp.where(position < stop, win_ref[brick] - first_window, trash)
-            offset = off_ref[brick]
-            inside = jnp.bitwise_and(e_ref[pl.ds(j, 1), :], WIN - 1)
-            pick = one_hot_rows(inside)
-            cols = pl.ds(pl.multiple_of(j * BLK, BLK), BLK)
-            summed = lax.dot_general(pick, xt_ref[:, cols], NT, preferred_element_type=jnp.float32)
-            part = jnp.dot(summed.astype(jnp.bfloat16), w_ref[offset], preferred_element_type=jnp.float32)
-            results.append((window, part))
-        for window, part in results:
-            rows = pl.ds(pl.multiple_of(window * WIN, WIN), WIN)
-            acc[rows, :] += part
-        return carry
-
-    lax.fori_loop(0, (stop - start + UNROLL - 1) // UNROLL, body, 0)
+    def run(first, width, trips):
+        def body(u, carry):
+            results = []
+            for t in range(width):
+                position = first + u * width + t
+                j = order_ref[step * per_step + jnp.minimum(position, per_step - 1)]
+                brick = step * per_step + j
+                window = jnp.where(position < stop, win_ref[brick] - first_window, trash)
+                offset = off_ref[brick]
+                inside = jnp.bitwise_and(e_ref[pl.ds(j, 1), :], WIN - 1)
+                pick = one_hot_rows(inside)
+                cols = pl.ds(pl.multiple_of(j * BLK, BLK), BLK)
+                summed = lax.dot_general(pick, xt_ref[:, cols], NT, preferred_element_type=jnp.float32)
+                part = jnp.dot(summed.astype(jnp.bfloat16), w_ref[offset], preferred_element_type=jnp.float32)
+                results.append((window, part))
+            for window, part in results:
+                rows = pl.ds(pl.multiple_of(window * WIN, WIN), WIN)
+                acc[rows, :] += part
+            return carry
+
+        lax.fori_loop(0, trips, body, 0)
+
+    run(start, UNROLL, (stop - start + UNROLL - 1) // UNROLL)
 
     @pl.when(step == pl.num_programs(0) - 1)
     def _():
@@ -95,11 +99,12 @@
     base = 0
     for src in sources:
         count = src.shape[0] // WIN
-
-        def gather_body(u, carry, src=src, base=base):
+        unroll = min(WIN_UNROLL, count)
+
+        def gather_body(u, carry, src=src, base=base, unroll=unroll):
             results = []
-            for t in range(WIN_UNROLL):
-                j = u * WIN_UNROLL + t
+            for t in range(unroll):
+                j = u * unroll + t
                 pick, rows = pick_of(base + j)
                 entries = src[pl.ds(pl.multiple_of(j * WIN, WIN), WIN), :]
                 results.append((rows, jnp.dot(pick, entries, preferred_element_type=jnp.float32)))
@@ -107,7 +112,7 @@
                 acc[rows, :] += value
             return carry
 
-        lax.fori_loop(0, count // WIN_UNROLL, gather_body, 0)
+        lax.fori_loop(0, count // unroll, gather_body, 0)
         base += count
 
     coarse[...] = jnp.maximum(acc[...] + bias_ref[...], 0.0).astype(jnp.bfloat16)
@@ -115,16 +120,17 @@
     base = 0
     for out in outs:
         count = out.shape[1] // WIN
-
-        def scatter_body(u, carry, out=out, base=base):
-            for t in range(WIN_UNROLL):
-                j = u * WIN_UNROLL + t
+        unroll = min(WIN_UNROLL, count)
+
+        def scatter_body(u, carry, out=out, base=base, unroll=unroll):
+            for t in range(unroll):
+                j = u * unroll + t
                 pick, rows = pick_of(base + j)
                 chosen = lax.dot_general(coarse[rows, :], pick, TN, preferred_element_type=jnp.float32)
                 out[:, pl.ds(pl.multiple_of(j * WIN, WIN), WIN)] = chosen.astype(jnp.bfloat16)
             return carry
 
-        lax.fori_loop(0, count // WIN_UNROLL, scatter_body, 0)
+        lax.fori_loop(0, count // unroll, scatter_body, 0)
         base += count
 
 
@@ -159,8 +165,8 @@
         out_ref[...] = prev_ref[...]
 
     def body(u, carry):
-        for t in range(UNROLL):
-            position = jnp.minimum(start + u * UNROLL + t, stop - 1)
+        for t in range(SPLIT_UNROLL):
+            position = jnp.minimum(start + u * SPLIT_UNROLL + t, stop - 1)
             j = order_ref[step * per_step + position]
             brick = step * per_step + j
             window = win_ref[brick] - first_window
@@ -174,7 +180,7 @@
             out_ref[:, cols] = (xt_ref[:, cols].astype(jnp.float32) + lifted).astype(out_ref.dtype)
         return carry
 
-    lax.fori_loop(0, (stop - start + UNROLL - 1) // UNROLL, body, 0)
+    lax.fori_loop(0, (stop - start + SPLIT_UNROLL - 1) // SPLIT_UNROLL, body, 0)
 
 
 def group_route(g, sign):

time: 103 us -> 88.4 us (0.86)
  Pallas kernels: 60.2 us -> 46.6 us
  starting transfers between devices: 26 us -> 18.1 us
  waiting for transfers between devices: 8.98 us -> 16.4 us
    pallas_call x2, Pallas kernels: 26.2 us -> 19.8 us  [down_call(): pl.pallas_call(functools.partial(down_kernel, first_window), out_shape=sh...]
    ppermute x8, starting transfers between devices: 14.3 us -> 8.17 us  [local(): lax.ppermute(answers[1 + g], ('outer', 'inner'), group_route(g, -1))]
    ppermute x8, waiting for transfers between devices: 4.77 us -> 9.42 us  [local(): lax.ppermute(answers[1 + g], ('outer', 'inner'), group_route(g, -1))]
    ppermute x8, waiting for transfers between devices: 4.21 us -> 6.99 us  [local(): lax.ppermute(parts[1 + g], ('outer', 'inner'), group_route(g, 1))]
    pallas_call x1, Pallas kernels: 12 us -> 9.33 us  [local(): own_up(counts, order, brick_window, block_offset, xt, entry_rows, w_up_t,...]
    pallas_call x1, Pallas kernels: 14 us -> 11.5 us  [local(): far_up(counts, order, brick_window, block_offset, xt, entry_rows, w_up_t,...]
    pallas_call x1, Pallas kernels: 8 us -> 6.03 us  [local(): coarse(cell_window, cells, b_down.reshape(1, out_width), parts[0], *arrived)]
    ppermute x8, starting transfers between devices: 11.7 us -> 9.97 us  [local(): lax.ppermute(parts[1 + g], ('outer', 'inner'), group_route(g, 1))]
  transfers between devices with their start and end apart: 16 -> 16, of which waited for: 6 -> 7; matrix products, arithmetic and copies ran while one was open for 1% -> 1% of each run, Pallas kernels for 25% -> 22%
where the time goes in v1:
time: 88.4 us; the launch traced here: 87.3 us
  Pallas kernels  46.6 us (53%)
  starting transfers between devices  18.1 us (20%)
  waiting for transfers between devices  16.4 us (19%)
  local copies, waits for them, and re-layouts  3.77 us (4%)
  other arithmetic  2.12 us (2%)
    pallas_call x2, Pallas kernels, down_call(): pl.pallas_call(functools.partial(down_kernel, first_window), out_shape=sh...  19.8 us
    pallas_call x1, Pallas kernels, local(): far_up(counts, order, brick_window, block_offset, xt, entry_rows, w_up_t,...  11.5 us
    ppermute x8, starting transfers between devices, local(): lax.ppermute(parts[1 + g], ('outer', 'inner'), group_route(g, 1))  9.97 us
    ppermute x8, waiting for transfers between devices, local(): lax.ppermute(answers[1 + g], ('outer', 'inner'), group_route(g, -1))  9.42 us
    pallas_call x1, Pallas kernels, local(): own_up(counts, order, brick_window, block_offset, xt, entry_rows, w_up_t,...  9.33 us
    ppermute x8, starting transfers between devices, local(): lax.ppermute(answers[1 + g], ('outer', 'inner'), group_route(g, -1))  8.17 us
    ppermute x8, waiting for transfers between devices, local(): lax.ppermute(parts[1 + g], ('outer', 'inner'), group_route(g, 1))  6.99 us
    pallas_call x1, Pallas kernels, local(): coarse(cell_window, cells, b_down.reshape(1, out_width), parts[0], *arrived)  6.03 us
  transfers between devices with their start and end apart: 16, of which 7 were waited for; matrix products, arithmetic and copies ran while one was open for 1% of the time, Pallas kernels for 22%

profile of v1, /device:TPU:24, one launch (start us, length us, event | category | flops | bytes accessed | tf_op | source)
XLA Modules:
  0.0 87.3 jit_solution(11242667896510295558)
XLA Ops:
  0.0 1.0 %slice_reduce_fusion = s32[256]{0:T(256)S(1)} fusion(s32[256,128]{1,0:T(8,128)} %bitcast.10), kind=kLoop, calls=%fused_computation | loop fusion | bytes 2048 | tf_op jit(solution)/shard_map/slice | solution.py:209
  1.0 0.6 and_select_fusion.1.win_ref
  1.6 0.1 squeeze.5
  1.7 0.1 convert_reduce_fusion.count_ref
  1.9 0.2 reduce_window_sum.18
  2.1 0.2 reduce_window_sum.17
  2.3 0.1 fusion.2
  2.4 0.1 select_reduce_fusion
  2.6 0.7 reshape.112.order_ref
  3.2 0.0 copy-done.17
  3.2 9.9 %shard_map.74 = (bf16[512,128]{1,0:T(8,128)(2,1)}, bf16[512,128]{1,0:T(8,128)(2,1)}, bf16[512,128]{1,0:T(8,128)(2,1)}, bf16[512,128]{1,0:T(8,128)(2,1)}, bf16[51...) custom-call(s32[4]{0:T(128)} %copy-done.17, ...), custom_call_target="tpu_custom_call" | custom-call | flops 536870912 | bytes 5373952 | tf_op jit(solution)/shard_map/pallas_call | solution.py:234
  13.1 5.9 %collective-permute-start = (bf16[512,128]{1,0:T(8,128)(2,1)}, bf16[512,128]{1,0:T(8,128)(2,1)S(1)}, u32[]{:S(2)}, u32[]{:S(2)}) collective-permute-start(bf16[512,128]{1,0:T(8,128)(2,1)} %get-tuple-element.22), channel_id=1, source_target_pairs={{0,127},{1,120},{2,121},{3,122},{4,123},{5,124},{6,125},{7,126},{8... | collective-permute-start | bytes 393224 | tf_op jit(solution)/shard_map/ppermute | solution.py:260
  19.0 0.2 collective-permute-start.1
  19.1 1.0 %collective-permute-start.2 = (bf16[512,128]{1,0:T(8,128)(2,1)}, bf16[512,128]{1,0:T(8,128)(2,1)S(1)}, u32[]{:S(2)}, u32[]{:S(2)}) collective-permute-start(bf16[512,128]{1,0:T(8,128)(2,1)} %get-tuple-element.24), channel_id=1, source_target_pairs={{0,121},{1,122},{2,123},{3,124},{4,125},{5,126},{6,127},{7,120},{8... | collective-permute-start | bytes 393224 | tf_op jit(solution)/shard_map/ppermute | solution.py:260
  20.1 0.7 collective-permute-start.3
  20.9 1.6 %collective-permute-start.4 = (bf16[512,128]{1,0:T(8,128)(2,1)}, bf16[512,128]{1,0:T(8,128)(2,1)S(1)}, u32[]{:S(2)}, u32[]{:S(2)}) collective-permute-start(bf16[512,128]{1,0:T(8,128)(2,1)} %get-tuple-element.26), channel_id=1, source_target_pairs={{0,1},{1,2},{2,3},{3,4},{4,5},{5,6},{6,7},{7,0},{8,9},{9,10},{10,1... | collective-permute-start | bytes 393224 | tf_op jit(solution)/shard_map/ppermute | solution.py:260
  22.5 0.0 copy-done.8
  22.5 0.1 reduce_min.9
  22.6 0.5 collective-permute-done.refs_1_
  23.1 0.6 collective-permute-start.5
  23.7 2.2 %collective-permute-done.1.refs_2_ = bf16[512,128]{1,0:T(8,128)(2,1)S(1)} collective-permute-done((bf16[512,128]{1,0:T(8,128)(2,1)}, bf16[512,128]{1,0:T(8,128)(2,1)S(1)}, u32[]{:S(2)}, u32[]{:S(2)}) %collective-permute-start.1) | collective-permute-done | bytes 131104 | tf_op jit(solution)/shard_map/ppermute | solution.py:260
  26.0 0.0 collective-permute-start.6
  26.0 2.6 %collective-permute-done.2.refs_3_ = bf16[512,128]{1,0:T(8,128)(2,1)S(1)} collective-permute-done((bf16[512,128]{1,0:T(8,128)(2,1)}, bf16[512,128]{1,0:T(8,128)(2,1)S(1)}, u32[]{:S(2)}, u32[]{:S(2)}) %collective-permute-start.2) | collective-permute-done | bytes 131104 | tf_op jit(solution)/shard_map/ppermute | solution.py:260
  28.5 0.0 collective-permute-start.7
  28.5 0.6 and_select_fusion.cw_ref
  29.1 9.9 %shard_map.73.refs_0_ = bf16[4096,128]{1,0:T(8,128)(2,1)} custom-call(s32[4]{0:T(128)} %copy-done.17, s32[256]{0:T(256)} %reshape.112.order_ref, s32[256]{0:T(256)} %and_select_fusion.1.win_ref, s32[256]{0:T(256)} %off_ref.7, bf16[64,32768]{1,0:T(8,128)(2,1)} %bitcast.7, s32[256,128]{1,0:T(8,128)} %bitcast.12, bf16[8,64,128]{2,1,0:T(8,128)(2,1)} %w_ref.3), custom_call_target="tpu_custom_call" | custom-call | flops 536870912 | bytes 5373952 | tf_op jit(solution)/shard_map/pallas_call | solution.py:234
  39.0 0.0 collective-permute-done.3.refs_4_
  39.0 0.0 collective-permute-done.4.refs_5_
  39.0 0.0 copy-start.13
  39.0 0.0 collective-permute-done.5.refs_6_
  39.0 0.0 copy-start.14
  39.0 0.0 collective-permute-done.6.refs_7_
  39.0 0.0 copy-start.15
  39.0 1.7 %collective-permute-done.7.refs_8_ = bf16[512,128]{1,0:T(8,128)(2,1)S(1)} collective-permute-done((bf16[512,128]{1,0:T(8,128)(2,1)}, bf16[512,128]{1,0:T(8,128)(2,1)S(1)}, u32[]{:S(2)}, u32[]{:S(2)}) %collective-permute-start.7) | collective-permute-done | bytes 131104 | tf_op jit(solution)/shard_map/ppermute | solution.py:260
  40.7 0.0 copy-done.9
  40.7 0.0 copy-done.10
  40.7 0.0 copy-done.11
  40.7 0.0 copy-done.12
  40.8 0.6 copy-done.16
  41.3 6.0 %shard_map.75 = (bf16[128,4096]{1,0:T(8,128)(2,1)}, bf16[128,512]{1,0:T(8,128)(2,1)}, bf16[128,512]{1,0:T(8,128)(2,1)}, bf16[128,512]{1,0:T(8,128)(2,1)}, bf16[1...) custom-call(s32[64]{0:T(128)} %and_select_fusion.cw_ref, ...), custom_call_target="tpu_custom_call" | custom-call | flops 536870912 | bytes 4194304 | tf_op jit(solution)/shard_map/pallas_call | solution.py:283
  47.4 0.0 collective-permute-start.8
  47.4 1.1 %collective-permute-start.9 = (bf16[128,512]{1,0:T(8,128)(2,1)}, bf16[128,512]{1,0:T(8,128)(2,1)S(1)}, u32[]{:S(2)}, u32[]{:S(2)}) collective-permute-start(bf16[128,512]{1,0:T(8,128)(2,1)} %get-tuple-element.31), channel_id=1, source_target_pairs={{120,0},{121,1},{122,2},{123,3},{124,4},{125,5},{126,6},{127,7},{0... | collective-permute-start | bytes 393224 | tf_op jit(solution)/shard_map/ppermute | solution.py:286
  48.5 1.3 %collective-permute-start.10 = (bf16[128,512]{1,0:T(8,128)(2,1)}, bf16[128,512]{1,0:T(8,128)(2,1)S(1)}, u32[]{:S(2)}, u32[]{:S(2)}) collective-permute-start(bf16[128,512]{1,0:T(8,128)(2,1)} %get-tuple-element.32), channel_id=1, source_target_pairs={{121,0},{122,1},{123,2},{124,3},{125,4},{126,5},{127,6},{120,7},{1... | collective-permute-start | bytes 393224 | tf_op jit(solution)/shard_map/ppermute | solution.py:286
  49.8 0.0 collective-permute-start.11
  49.8 1.7 %collective-permute-start.12 = (bf16[128,512]{1,0:T(8,128)(2,1)}, bf16[128,512]{1,0:T(8,128)(2,1)S(1)}, u32[]{:S(2)}, u32[]{:S(2)}) collective-permute-start(bf16[128,512]{1,0:T(8,128)(2,1)} %get-tuple-element.34), channel_id=1, source_target_pairs={{1,0},{2,1},{3,2},{4,3},{5,4},{6,5},{7,6},{0,7},{9,8},{10,9},{11,1... | collective-permute-start | bytes 393224 | tf_op jit(solution)/shard_map/ppermute | solution.py:286
  51.5 6.0 %collective-permute-done.8.refs_0_ = bf16[128,512]{1,0:T(8,128)(2,1)S(1)} collective-permute-done((bf16[128,512]{1,0:T(8,128)(2,1)}, bf16[128,512]{1,0:T(8,128)(2,1)S(1)}, u32[]{:S(2)}, u32[]{:S(2)}) %collective-permute-start.8) | collective-permute-done | bytes 131104 | tf_op jit(solution)/shard_map/ppermute | solution.py:286
  57.6 1.0 %collective-permute-start.13 = (bf16[128,512]{1,0:T(8,128)(2,1)}, bf16[128,512]{1,0:T(8,128)(2,1)S(1)}, u32[]{:S(2)}, u32[]{:S(2)}) collective-permute-start(bf16[128,512]{1,0:T(8,128)(2,1)} %get-tuple-element.35), channel_id=1, source_target_pairs={{15,0},{8,1},{9,2},{10,3},{11,4},{12,5},{13,6},{14,7},{23,8},{16,9... | collective-permute-start | bytes 393224 | tf_op jit(solution)/shard_map/ppermute | solution.py:286
  58.6 1.8 %collective-permute-done.9.refs_1_ = bf16[128,512]{1,0:T(8,128)(2,1)S(1)} collective-permute-done((bf16[128,512]{1,0:T(8,128)(2,1)}, bf16[128,512]{1,0:T(8,128)(2,1)S(1)}, u32[]{:S(2)}, u32[]{:S(2)}) %collective-permute-start.9) | collective-permute-done | bytes 131104 | tf_op jit(solution)/shard_map/ppermute | solution.py:286
  60.4 1.3 %collective-permute-start.14 = (bf16[128,512]{1,0:T(8,128)(2,1)}, bf16[128,512]{1,0:T(8,128)(2,1)S(1)}, u32[]{:S(2)}, u32[]{:S(2)}) collective-permute-start(bf16[128,512]{1,0:T(8,128)(2,1)} %get-tuple-element.36), channel_id=1, source_target_pairs={{8,0},{9,1},{10,2},{11,3},{12,4},{13,5},{14,6},{15,7},{16,8},{17,9... | collective-permute-start | bytes 393224 | tf_op jit(solution)/shard_map/ppermute | solution.py:286
  61.7 1.6 %collective-permute-done.10.refs_2_ = bf16[128,512]{1,0:T(8,128)(2,1)S(1)} collective-permute-done((bf16[128,512]{1,0:T(8,128)(2,1)}, bf16[128,512]{1,0:T(8,128)(2,1)S(1)}, u32[]{:S(2)}, u32[]{:S(2)}) %collective-permute-start.10) | collective-permute-done | bytes 131104 | tf_op jit(solution)/shard_map/ppermute | solution.py:286
  63.3 1.6 %collective-permute-start.15 = (bf16[128,512]{1,0:T(8,128)(2,1)}, bf16[128,512]{1,0:T(8,128)(2,1)S(1)}, u32[]{:S(2)}, u32[]{:S(2)}) collective-permute-start(bf16[128,512]{1,0:T(8,128)(2,1)} %get-tuple-element.37), channel_id=1, source_target_pairs={{9,0},{10,1},{11,2},{12,3},{13,4},{14,5},{15,6},{8,7},{17,8},{18,9... | collective-permute-start | bytes 393224 | tf_op jit(solution)/shard_map/ppermute | solution.py:286
  65.0 9.3 %shard_map.76.refs_8_ = bf16[64,32768]{1,0:T(8,128)(2,1)} custom-call(s32[4]{0:T(128)} %copy-done.17, s32[256]{0:T(256)} %reshape.112.order_ref, s32[256]{0:T(256)} %and_select_fusion.1.win_ref, s32[256]{0:T(256)} %off_ref.7, bf16[64,32768]{1,0:T(8,128)(2,1)} %bitcast.8, s32[256,128]{1,0:T(8,128)} %bitcast.13, bf16[8,64,128]{2,1,0:T(8,128)(2,1)} %bitcast.15, ...), custom_call_target="tpu_custom_call" | custom-call | flops 536870912 | bytes 4259840 | tf_op jit(solution)/shard_map/pallas_call | solution.py:309
  74.3 0.0 collective-permute-done.11.refs_3_
  74.3 0.0 collective-permute-done.12.refs_4_
  74.4 0.0 copy-start.4
  74.4 0.0 collective-permute-done.13.refs_5_
  74.4 0.0 collective-permute-done.14.refs_6_
  74.4 0.0 collective-permute-done.15.refs_7_
  74.4 0.6 copy-done.3
  75.0 0.1 copy-done.4
  75.0 0.1 copy-done.5
  75.1 0.0 copy-done.6
  75.1 0.6 copy-done.7
  75.8 11.5 %shard_map.77 = bf16[64,32768]{1,0:T(8,128)(2,1)} custom-call(s32[4]{0:T(128)} %copy-done.17, s32[256]{0:T(256)} %reshape.112.order_ref, s32[256]{0:T(256)} %and_select_fusion.1.win_ref, s32[256]{0:T(256)} %off_ref.7, bf16[64,32768]{1,0:T(8,128)(2,1)} %bitcast.9, s32[256,128]{1,0:T(8,128)} %bitcast.14, ...), custom_call_target="tpu_custom_call", output_to_operand_aliasing={{}: (15, {})} | custom-call | flops 536870912 | bytes 4259840 | tf_op jit(solution)/shard_map/pallas_call | solution.py:330
  (22 shorter events, 0.1 us)
Async XLA Ops:
  0.0 22.5 %copy-start.8 = (s32[1,8192]{1,0:T(1,128)S(1)}, s32[1,8192]{1,0:T(1,128)}, u32[]{:S(2)}) copy-start(s32[1,8192]{1,0:T(1,128)} %param.10) | copy-start | bytes 98308
  1.8 1.4 %copy-start.17 = (s32[4]{0:T(128)}, s32[4]{0:T(128)S(1)}, u32[]{:S(2)}) copy-start(s32[4]{0:T(128)S(1)} %convert_reduce_fusion.count_ref) | copy-start | bytes 52
  13.1 10.0 %collective-permute-start = (bf16[512,128]{1,0:T(8,128)(2,1)}, bf16[512,128]{1,0:T(8,128)(2,1)S(1)}, u32[]{:S(2)}, u32[]{:S(2)}) collective-permute-start(bf16[512,128]{1,0:T(8,128)(2,1)} %get-tuple-element.22), channel_id=1, source_target_pairs={{0,127},{1,120},{2,121},{3,122},{4,123},{5,124},{6,125},{7,126},{8... | collective-permute-start | bytes 393224 | tf_op jit(solution)/shard_map/ppermute | solution.py:260
  19.0 7.0 %collective-permute-start.1 = (bf16[512,128]{1,0:T(8,128)(2,1)}, bf16[512,128]{1,0:T(8,128)(2,1)S(1)}, u32[]{:S(2)}, u32[]{:S(2)}) collective-permute-start(bf16[512,128]{1,0:T(8,128)(2,1)} %get-tuple-element.23), channel_id=1, source_target_pairs={{0,120},{1,121},{2,122},{3,123},{4,124},{5,125},{6,126},{7,127},{8... | collective-permute-start | bytes 393224 | tf_op jit(solution)/shard_map/ppermute | solution.py:260
  19.1 9.4 %collective-permute-start.2 = (bf16[512,128]{1,0:T(8,128)(2,1)}, bf16[512,128]{1,0:T(8,128)(2,1)S(1)}, u32[]{:S(2)}, u32[]{:S(2)}) collective-permute-start(bf16[512,128]{1,0:T(8,128)(2,1)} %get-tuple-element.24), channel_id=1, source_target_pairs={{0,121},{1,122},{2,123},{3,124},{4,125},{5,126},{6,127},{7,120},{8... | collective-permute-start | bytes 393224 | tf_op jit(solution)/shard_map/ppermute | solution.py:260
  20.1 18.8 %collective-permute-start.3 = (bf16[512,128]{1,0:T(8,128)(2,1)}, bf16[512,128]{1,0:T(8,128)(2,1)S(1)}, u32[]{:S(2)}, u32[]{:S(2)}) collective-permute-start(bf16[512,128]{1,0:T(8,128)(2,1)} %get-tuple-element.25), channel_id=1, source_target_pairs={{0,7},{1,0},{2,1},{3,2},{4,3},{5,4},{6,5},{7,6},{8,15},{9,8},{10,9... | collective-permute-start | bytes 393224 | tf_op jit(solution)/shard_map/ppermute | solution.py:260
  20.9 18.1 %collective-permute-start.4 = (bf16[512,128]{1,0:T(8,128)(2,1)}, bf16[512,128]{1,0:T(8,128)(2,1)S(1)}, u32[]{:S(2)}, u32[]{:S(2)}) collective-permute-start(bf16[512,128]{1,0:T(8,128)(2,1)} %get-tuple-element.26), channel_id=1, source_target_pairs={{0,1},{1,2},{2,3},{3,4},{4,5},{5,6},{6,7},{7,0},{8,9},{9,10},{10,1... | collective-permute-start | bytes 393224 | tf_op jit(solution)/shard_map/ppermute | solution.py:260
  23.1 17.6 %copy-start.9 = (bf16[512,128]{1,0:T(8,128)(2,1)}, bf16[512,128]{1,0:T(8,128)(2,1)S(1)}, u32[]{:S(2)}) copy-start(bf16[512,128]{1,0:T(8,128)(2,1)S(1)} %collective-permute-done.refs_1_) | copy-start | bytes 393220
  23.1 15.9 %collective-permute-start.5 = (bf16[512,128]{1,0:T(8,128)(2,1)}, bf16[512,128]{1,0:T(8,128)(2,1)S(1)}, u32[]{:S(2)}, u32[]{:S(2)}) collective-permute-start(bf16[512,128]{1,0:T(8,128)(2,1)} %get-tuple-element.27), channel_id=1, source_target_pairs={{0,15},{1,8},{2,9},{3,10},{4,11},{5,12},{6,13},{7,14},{8,23},{9,16... | collective-permute-start | bytes 393224 | tf_op jit(solution)/shard_map/ppermute | solution.py:260
  26.0 14.8 %copy-start.10 = (bf16[512,128]{1,0:T(8,128)(2,1)}, bf16[512,128]{1,0:T(8,128)(2,1)S(1)}, u32[]{:S(2)}) copy-start(bf16[512,128]{1,0:T(8,128)(2,1)S(1)} %collective-permute-done.1.refs_2_) | copy-start | bytes 393220
  26.0 13.1 %collective-permute-start.6 = (bf16[512,128]{1,0:T(8,128)(2,1)}, bf16[512,128]{1,0:T(8,128)(2,1)S(1)}, u32[]{:S(2)}, u32[]{:S(2)}) collective-permute-start(bf16[512,128]{1,0:T(8,128)(2,1)} %get-tuple-element.28), channel_id=1, source_target_pairs={{0,8},{1,9},{2,10},{3,11},{4,12},{5,13},{6,14},{7,15},{8,16},{9,17... | collective-permute-start | bytes 393224 | tf_op jit(solution)/shard_map/ppermute | solution.py:260
  28.5 12.2 %copy-start.11 = (bf16[512,128]{1,0:T(8,128)(2,1)}, bf16[512,128]{1,0:T(8,128)(2,1)S(1)}, u32[]{:S(2)}) copy-start(bf16[512,128]{1,0:T(8,128)(2,1)S(1)} %collective-permute-done.2.refs_3_) | copy-start | bytes 393220
  28.5 12.2 %collective-permute-start.7 = (bf16[512,128]{1,0:T(8,128)(2,1)}, bf16[512,128]{1,0:T(8,128)(2,1)S(1)}, u32[]{:S(2)}, u32[]{:S(2)}) collective-permute-start(bf16[512,128]{1,0:T(8,128)(2,1)} %get-tuple-element.29), channel_id=1, source_target_pairs={{0,9},{1,10},{2,11},{3,12},{4,13},{5,14},{6,15},{7,8},{8,17},{9,18... | collective-permute-start | bytes 393224 | tf_op jit(solution)/shard_map/ppermute | solution.py:260
  39.0 1.7 %copy-start.12 = (bf16[512,128]{1,0:T(8,128)(2,1)}, bf16[512,128]{1,0:T(8,128)(2,1)S(1)}, u32[]{:S(2)}) copy-start(bf16[512,128]{1,0:T(8,128)(2,1)S(1)} %collective-permute-done.3.refs_4_) | copy-start | bytes 393220
  39.0 1.7 %copy-start.13 = (bf16[512,128]{1,0:T(8,128)(2,1)}, bf16[512,128]{1,0:T(8,128)(2,1)S(1)}, u32[]{:S(2)}) copy-start(bf16[512,128]{1,0:T(8,128)(2,1)S(1)} %collective-permute-done.4.refs_5_) | copy-start | bytes 393220
  39.0 1.7 %copy-start.14 = (bf16[512,128]{1,0:T(8,128)(2,1)}, bf16[512,128]{1,0:T(8,128)(2,1)S(1)}, u32[]{:S(2)}) copy-start(bf16[512,128]{1,0:T(8,128)(2,1)S(1)} %collective-permute-done.5.refs_6_) | copy-start | bytes 393220
  39.0 1.7 %copy-start.15 = (bf16[512,128]{1,0:T(8,128)(2,1)}, bf16[512,128]{1,0:T(8,128)(2,1)S(1)}, u32[]{:S(2)}) copy-start(bf16[512,128]{1,0:T(8,128)(2,1)S(1)} %collective-permute-done.6.refs_7_) | copy-start | bytes 393220
  40.7 0.6 copy-start.16
  47.4 10.2 %collective-permute-start.8 = (bf16[128,512]{1,0:T(8,128)(2,1)}, bf16[128,512]{1,0:T(8,128)(2,1)S(1)}, u32[]{:S(2)}, u32[]{:S(2)}) collective-permute-start(bf16[128,512]{1,0:T(8,128)(2,1)} %get-tuple-element.30), channel_id=1, source_target_pairs={{127,0},{120,1},{121,2},{122,3},{123,4},{124,5},{125,6},{126,7},{7... | collective-permute-start | bytes 393224 | tf_op jit(solution)/shard_map/ppermute | solution.py:286
  47.4 13.0 %collective-permute-start.9 = (bf16[128,512]{1,0:T(8,128)(2,1)}, bf16[128,512]{1,0:T(8,128)(2,1)S(1)}, u32[]{:S(2)}, u32[]{:S(2)}) collective-permute-start(bf16[128,512]{1,0:T(8,128)(2,1)} %get-tuple-element.31), channel_id=1, source_target_pairs={{120,0},{121,1},{122,2},{123,3},{124,4},{125,5},{126,6},{127,7},{0... | collective-permute-start | bytes 393224 | tf_op jit(solution)/shard_map/ppermute | solution.py:286
  48.5 14.9 %collective-permute-start.10 = (bf16[128,512]{1,0:T(8,128)(2,1)}, bf16[128,512]{1,0:T(8,128)(2,1)S(1)}, u32[]{:S(2)}, u32[]{:S(2)}) collective-permute-start(bf16[128,512]{1,0:T(8,128)(2,1)} %get-tuple-element.32), channel_id=1, source_target_pairs={{121,0},{122,1},{123,2},{124,3},{125,4},{126,5},{127,6},{120,7},{1... | collective-permute-start | bytes 393224 | tf_op jit(solution)/shard_map/ppermute | solution.py:286
  49.8 24.5 %collective-permute-start.11 = (bf16[128,512]{1,0:T(8,128)(2,1)}, bf16[128,512]{1,0:T(8,128)(2,1)S(1)}, u32[]{:S(2)}, u32[]{:S(2)}) collective-permute-start(bf16[128,512]{1,0:T(8,128)(2,1)} %get-tuple-element.33), channel_id=1, source_target_pairs={{7,0},{0,1},{1,2},{2,3},{3,4},{4,5},{5,6},{6,7},{15,8},{8,9},{9,10... | collective-permute-start | bytes 393224 | tf_op jit(solution)/shard_map/ppermute | solution.py:286
  49.8 24.5 %collective-permute-start.12 = (bf16[128,512]{1,0:T(8,128)(2,1)}, bf16[128,512]{1,0:T(8,128)(2,1)S(1)}, u32[]{:S(2)}, u32[]{:S(2)}) collective-permute-start(bf16[128,512]{1,0:T(8,128)(2,1)} %get-tuple-element.34), channel_id=1, source_target_pairs={{1,0},{2,1},{3,2},{4,3},{5,4},{6,5},{7,6},{0,7},{9,8},{10,9},{11,1... | collective-permute-start | bytes 393224 | tf_op jit(solution)/shard_map/ppermute | solution.py:286
  57.6 16.7 %copy-start = (bf16[128,512]{1,0:T(8,128)(2,1)}, bf16[128,512]{1,0:T(8,128)(2,1)S(1)}, u32[]{:S(2)}) copy-start(bf16[128,512]{1,0:T(8,128)(2,1)S(1)} %collective-permute-done.8.refs_0_) | copy-start | bytes 393220
  57.6 16.8 %collective-permute-start.13 = (bf16[128,512]{1,0:T(8,128)(2,1)}, bf16[128,512]{1,0:T(8,128)(2,1)S(1)}, u32[]{:S(2)}, u32[]{:S(2)}) collective-permute-start(bf16[128,512]{1,0:T(8,128)(2,1)} %get-tuple-element.35), channel_id=1, source_target_pairs={{15,0},{8,1},{9,2},{10,3},{11,4},{12,5},{13,6},{14,7},{23,8},{16,9... | collective-permute-start | bytes 393224 | tf_op jit(solution)/shard_map/ppermute | solution.py:286
  60.4 13.9 %copy-start.1 = (bf16[128,512]{1,0:T(8,128)(2,1)}, bf16[128,512]{1,0:T(8,128)(2,1)S(1)}, u32[]{:S(2)}) copy-start(bf16[128,512]{1,0:T(8,128)(2,1)S(1)} %collective-permute-done.9.refs_1_) | copy-start | bytes 393220
  60.4 14.0 %collective-permute-start.14 = (bf16[128,512]{1,0:T(8,128)(2,1)}, bf16[128,512]{1,0:T(8,128)(2,1)S(1)}, u32[]{:S(2)}, u32[]{:S(2)}) collective-permute-start(bf16[128,512]{1,0:T(8,128)(2,1)} %get-tuple-element.36), channel_id=1, source_target_pairs={{8,0},{9,1},{10,2},{11,3},{12,4},{13,5},{14,6},{15,7},{16,8},{17,9... | collective-permute-start | bytes 393224 | tf_op jit(solution)/shard_map/ppermute | solution.py:286
  63.3 11.0 %copy-start.2 = (bf16[128,512]{1,0:T(8,128)(2,1)}, bf16[128,512]{1,0:T(8,128)(2,1)S(1)}, u32[]{:S(2)}) copy-start(bf16[128,512]{1,0:T(8,128)(2,1)S(1)} %collective-permute-done.10.refs_2_) | copy-start | bytes 393220
  63.3 11.1 %collective-permute-start.15 = (bf16[128,512]{1,0:T(8,128)(2,1)}, bf16[128,512]{1,0:T(8,128)(2,1)S(1)}, u32[]{:S(2)}, u32[]{:S(2)}) collective-permute-start(bf16[128,512]{1,0:T(8,128)(2,1)} %get-tuple-element.37), channel_id=1, source_target_pairs={{9,0},{10,1},{11,2},{12,3},{13,4},{14,5},{15,6},{8,7},{17,8},{18,9... | collective-permute-start | bytes 393224 | tf_op jit(solution)/shard_map/ppermute | solution.py:286
  74.3 0.6 copy-start.3
  74.4 0.7 copy-start.4
  74.4 0.7 copy-start.5
  74.4 0.7 copy-start.6
  75.1 0.6 copy-start.7
